TPU v7x, 512 devices: a whole 4x8x8 slice. The times are simulated.
512 devices in a mesh: chain: 64 (over y, z), cross: 8 (over x, core).
Axes of the slice: x: 4, y: 8, z: 8, core: 2. Of those that a mesh axis runs over, the one named last changes fastest.
Arguments:
- right_side: bfloat16 [64, 1024, 512], P('chain', 'cross'), may hold values from -6 to 6
- self_factor: bfloat16 [6, 64, 1024, 1024], P(None, 'chain', 'cross')
- lower_factor: bfloat16 [6, 64, 1024, 1024], P(None, 'chain', 'cross'), may hold values from -0.078125 to 0.078125
- upper_factor: bfloat16 [6, 64, 1024, 1024], P(None, 'chain', 'cross'), may hold values from -0.078125 to 0.078125
Outputs:
- solution: bfloat16 [64, 1024, 512], P('chain', 'cross')
All inputs are finite; a program needn't handle non-finite values.
Results may differ from a plain program's by a relative error of at most 0.014.
Values may be sent and summed in bfloat16 or wider, within the bound.
No kernel may reach another device: no remote copies, remote signals or barrier semaphores. Data moves between devices by JAX's collectives and lax.ppermute only.
A program may use at most 64 MiB of HBM per device.

v0:
```python
import jax
import jax.numpy as jnp
from jax import lax
from jax.sharding import PartitionSpec as P


def shifted(value, axis, steps):
    count = lax.axis_size(axis)
    initial, last = (max(0, -steps), min(count, count - steps))
    return lax.ppermute(value, axis, [(source, source + steps) for source in range(initial, last)])


def reach_full(piece, dist):
    lower = shifted(piece, "chain", dist)
    upper = shifted(piece, "chain", -dist)
    return (lower, upper)


def body(right_side, self_factor, lower_factor, upper_factor):
    levels = lax.axis_size("chain").bit_length() - 1
    current = right_side[0]
    for level in range(levels):
        dist = 2**level
        own_mat = self_factor[level, 0]
        low_mat = lower_factor[level, 0]
        up_mat = upper_factor[level, 0]
        whole = lax.all_gather(current, "cross", axis=0, tiled=True)
        lower, upper = reach_full(whole, dist)
        total = jnp.dot(own_mat, whole, preferred_element_type=jnp.float32)
        total = total - jnp.dot(low_mat, lower, preferred_element_type=jnp.float32)
        total = total - jnp.dot(up_mat, upper, preferred_element_type=jnp.float32)
        current = total.astype(jnp.bfloat16)
    return current[None]


def solution(mesh):
    return jax.shard_map(
        body,
        mesh=mesh,
        in_specs=(
            P("chain", "cross", None),
            P(None, "chain", "cross", None),
            P(None, "chain", "cross", None),
            P(None, "chain", "cross", None),
        ),
        out_specs=P("chain", "cross", None),
        check_vma=False,
    )
```

profile of v0, /device:TPU:1, one launch (start us, length us, event | category | flops | bytes accessed | tf_op | source)
XLA Modules:
  0.0 539.7 jit_solution(4165311589859038631)
XLA Ops:
  6.5 0.7 all-gather.18.cloned.1.call-update
  7.3 37.0 %all-gather.18.cloned.1.call-done = bf16[1,1024,512]{2,1,0:T(8,128)(2,1)} async-done(((bf16[1,128,512]{2,1,0:T(8,128)(2,1)}), bf16[1,1024,512]{2,1,0:T(8,128)(2,1)}) %all-gather.18.cloned.1.call-update) | async-done | bytes 1048592 | tf_op jit(solution)/shard_map/all_gather | solution.py:27
  44.3 3.2 collective-permute-start
  47.5 1.3 collective-permute-start.1
  48.8 1.6 fusion.33
  50.4 19.6 %collective-permute-done = bf16[1024,512]{1,0:T(8,128)(2,1)S(1)} collective-permute-done((bf16[1024,512]{1,0:T(8,128)(2,1)}, bf16[1024,512]{1,0:T(8,128)(2,1)S(1)}, u32[]{:S(2)}, u32[]{:S(2)}) %collective-permute-start) | collective-permute-done | bytes 1048608 | tf_op jit(solution)/shard_map/ppermute | solution.py:10
  70.3 3.4 collective-permute-done.1
  73.8 1.9 fusion
  75.8 30.0 %all-gather.8.cloned.1.call-done = bf16[1024,512]{1,0:T(8,128)(2,1)} async-done(((bf16[128,512]{1,0:T(8,128)(2,1)}), bf16[1024,512]{1,0:T(8,128)(2,1)}) %all-gather.8.cloned.1.call-update) | async-done | bytes 1048592 | tf_op jit(solution)/shard_map/all_gather | solution.py:27
  105.8 4.2 collective-permute-start.2
  110.1 1.3 collective-permute-start.3
  111.4 1.7 fusion.29
  113.1 19.6 %collective-permute-done.2 = bf16[1024,512]{1,0:T(8,128)(2,1)S(1)} collective-permute-done((bf16[1024,512]{1,0:T(8,128)(2,1)}, bf16[1024,512]{1,0:T(8,128)(2,1)S(1)}, u32[]{:S(2)}, u32[]{:S(2)}) %collective-permute-start.2) | collective-permute-done | bytes 1048608 | tf_op jit(solution)/shard_map/ppermute | solution.py:10
  132.7 0.5 convolution_subtract_fusion.9
  133.1 30.1 %collective-permute-done.3 = bf16[1024,512]{1,0:T(8,128)(2,1)S(1)} collective-permute-done((bf16[1024,512]{1,0:T(8,128)(2,1)}, bf16[1024,512]{1,0:T(8,128)(2,1)S(1)}, u32[]{:S(2)}, u32[]{:S(2)}) %collective-permute-start.3) | collective-permute-done | bytes 1048608 | tf_op jit(solution)/shard_map/ppermute | solution.py:10
  163.2 2.1 fusion.10
  165.4 25.3 %all-gather.10.cloned.1.call-done = bf16[1024,512]{0,1:T(8,128)(2,1)} async-done(((bf16[128,512]{0,1:T(8,128)(2,1)}), bf16[1024,512]{0,1:T(8,128)(2,1)}) %all-gather.10.cloned.1.call-update) | async-done | bytes 1048592 | tf_op jit(solution)/shard_map/all_gather | solution.py:27
  190.7 7.8 %collective-permute-start.4 = (bf16[1024,512]{0,1:T(8,128)(2,1)}, bf16[1024,512]{0,1:T(8,128)(2,1)S(1)}, u32[]{:S(2)}, u32[]{:S(2)}) collective-permute-start(bf16[1024,512]{0,1:T(8,128)(2,1)} %all-gather.10.cloned.1.call-done), channel_id=1, source_target_pairs={{0,32},{8,40},{16,48},{24,56},{32,64},{40,72},{48,80},{56,88},{64,... | collective-permute-start | bytes 3145736 | tf_op jit(solution)/shard_map/ppermute | solution.py:10
  198.5 1.3 collective-permute-start.5
  199.8 1.7 fusion.25
  201.4 65.5 %collective-permute-done.4 = bf16[1024,512]{0,1:T(8,128)(2,1)S(1)} collective-permute-done((bf16[1024,512]{0,1:T(8,128)(2,1)}, bf16[1024,512]{0,1:T(8,128)(2,1)S(1)}, u32[]{:S(2)}, u32[]{:S(2)}) %collective-permute-start.4) | collective-permute-done | bytes 1048608 | tf_op jit(solution)/shard_map/ppermute | solution.py:10
  267.0 0.4 convolution_subtract_fusion.7
  267.4 2.0 fusion.9
  269.5 54.1 %all-gather.12.cloned.1.call-done = bf16[1024,512]{0,1:T(8,128)(2,1)} async-done(((bf16[128,512]{0,1:T(8,128)(2,1)}), bf16[1024,512]{0,1:T(8,128)(2,1)}) %all-gather.12.cloned.1.call-update) | async-done | bytes 1048592 | tf_op jit(solution)/shard_map/all_gather | solution.py:27
  323.7 3.2 collective-permute-start.6
  326.8 1.3 collective-permute-start.7
  328.1 1.7 fusion.21
  329.8 19.5 %collective-permute-done.6 = bf16[1024,512]{0,1:T(8,128)(2,1)S(1)} collective-permute-done((bf16[1024,512]{0,1:T(8,128)(2,1)}, bf16[1024,512]{0,1:T(8,128)(2,1)S(1)}, u32[]{:S(2)}, u32[]{:S(2)}) %collective-permute-start.6) | collective-permute-done | bytes 1048608 | tf_op jit(solution)/shard_map/ppermute | solution.py:10
  349.3 0.4 convolution_subtract_fusion.5
  349.8 3.3 collective-permute-done.7
  353.1 2.0 fusion.8
  355.2 31.2 %all-gather.14.cloned.1.call-done = bf16[1024,512]{0,1:T(8,128)(2,1)} async-done(((bf16[128,512]{0,1:T(8,128)(2,1)}), bf16[1024,512]{0,1:T(8,128)(2,1)}) %all-gather.14.cloned.1.call-update) | async-done | bytes 1048592 | tf_op jit(solution)/shard_map/all_gather | solution.py:27
  386.4 4.1 collective-permute-start.8
  390.5 1.3 collective-permute-start.9
  391.8 1.7 fusion.17
  393.5 19.6 %collective-permute-done.8 = bf16[1024,512]{0,1:T(8,128)(2,1)S(1)} collective-permute-done((bf16[1024,512]{0,1:T(8,128)(2,1)}, bf16[1024,512]{0,1:T(8,128)(2,1)S(1)}, u32[]{:S(2)}, u32[]{:S(2)}) %collective-permute-start.8) | collective-permute-done | bytes 1048608 | tf_op jit(solution)/shard_map/ppermute | solution.py:10
  413.1 0.4 convolution_subtract_fusion.3
  413.5 28.4 %collective-permute-done.9 = bf16[1024,512]{0,1:T(8,128)(2,1)S(1)} collective-permute-done((bf16[1024,512]{0,1:T(8,128)(2,1)}, bf16[1024,512]{0,1:T(8,128)(2,1)S(1)}, u32[]{:S(2)}, u32[]{:S(2)}) %collective-permute-start.9) | collective-permute-done | bytes 1048608 | tf_op jit(solution)/shard_map/ppermute | solution.py:10
  441.9 2.0 fusion.7
  444.0 28.5 %all-gather.16.cloned.1.call-done = bf16[1024,512]{0,1:T(8,128)(2,1)} async-done(((bf16[128,512]{0,1:T(8,128)(2,1)}), bf16[1024,512]{0,1:T(8,128)(2,1)}) %all-gather.16.cloned.1.call-update) | async-done | bytes 1048592 | tf_op jit(solution)/shard_map/all_gather | solution.py:27
  472.5 7.1 %collective-permute-start.10 = (bf16[1024,512]{0,1:T(8,128)(2,1)}, bf16[1024,512]{0,1:T(8,128)(2,1)S(1)}, u32[]{:S(2)}, u32[]{:S(2)}) collective-permute-start(bf16[1024,512]{0,1:T(8,128)(2,1)} %all-gather.16.cloned.1.call-done), channel_id=1, source_target_pairs={{0,256},{8,264},{16,272},{24,280},{32,288},{40,296},{48,304},{56,3... | collective-permute-start | bytes 3145736 | tf_op jit(solution)/shard_map/ppermute | solution.py:10
  479.7 1.3 collective-permute-start.11
  481.0 1.7 fusion.13
  482.6 32.1 %collective-permute-done.10 = bf16[1024,512]{0,1:T(8,128)(2,1)S(1)} collective-permute-done((bf16[1024,512]{0,1:T(8,128)(2,1)}, bf16[1024,512]{0,1:T(8,128)(2,1)S(1)}, u32[]{:S(2)}, u32[]{:S(2)}) %collective-permute-start.10) | collective-permute-done | bytes 1048608 | tf_op jit(solution)/shard_map/ppermute | solution.py:10
  514.7 0.4 convolution_subtract_fusion.1
  515.1 15.6 %collective-permute-done.11 = bf16[1024,512]{0,1:T(8,128)(2,1)S(1)} collective-permute-done((bf16[1024,512]{0,1:T(8,128)(2,1)}, bf16[1024,512]{0,1:T(8,128)(2,1)S(1)}, u32[]{:S(2)}, u32[]{:S(2)}) %collective-permute-start.11) | collective-permute-done | bytes 1048608 | tf_op jit(solution)/shard_map/ppermute | solution.py:10
  530.7 1.4 fusion.6
  532.1 0.8 copy.5
  (17 shorter events, 0.6 us)
Async XLA Ops:
  6.5 63.5 %copy-start = (bf16[6,1,128,1024]{3,2,1,0:T(8,128)(2,1)S(1)}, bf16[6,1,128,1024]{3,2,1,0:T(8,128)(2,1)}, u32[]{:S(2)}) copy-start(bf16[6,1,128,1024]{3,2,1,0:T(8,128)(2,1)} %param.6) | copy-start | bytes 4718596
  6.5 37.8 %all-gather.18.cloned.1.call-start = ((), (), s32[]{:S(2)}) async-start(), calls=%async_computation.5 | async-start | bytes 1179648 | tf_op jit(solution)/shard_map/all_gather | solution.py:27
  7.3 98.6 %all-gather.8.cloned.1.call-start = ((), (), s32[]{:S(2)}) async-start(), calls=%async_computation | async-start | bytes 1179648 | tf_op jit(solution)/shard_map/all_gather | solution.py:27
  44.3 25.7 %collective-permute-start = (bf16[1024,512]{1,0:T(8,128)(2,1)}, bf16[1024,512]{1,0:T(8,128)(2,1)S(1)}, u32[]{:S(2)}, u32[]{:S(2)}) collective-permute-start(bf16[1024,512]{1,0:T(8,128)(2,1)} %bitcast.86), channel_id=1, source_target_pairs={{0,8},{8,16},{16,24},{24,32},{32,40},{40,48},{48,56},{56,64},{64,7... | collective-permute-start | bytes 3145736 | tf_op jit(solution)/shard_map/ppermute | solution.py:10
  47.5 26.3 %collective-permute-start.1 = (bf16[1024,512]{1,0:T(8,128)(2,1)}, bf16[1024,512]{1,0:T(8,128)(2,1)S(1)}, u32[]{:S(2)}, u32[]{:S(2)}) collective-permute-start(bf16[1024,512]{1,0:T(8,128)(2,1)} %bitcast.87), channel_id=1, source_target_pairs={{8,0},{16,8},{24,16},{32,24},{40,32},{48,40},{56,48},{64,56},{72,6... | collective-permute-start | bytes 3145736 | tf_op jit(solution)/shard_map/ppermute | solution.py:10
  50.4 61.0 %copy-start.1 = (bf16[6,1,128,1024]{3,2,1,0:T(8,128)(2,1)S(1)}, bf16[6,1,128,1024]{3,2,1,0:T(8,128)(2,1)}, u32[]{:S(2)}) copy-start(bf16[6,1,128,1024]{3,2,1,0:T(8,128)(2,1)} %param.5) | copy-start | bytes 4718596
  75.7 115.0 %all-gather.10.cloned.1.call-start = ((), (), s32[]{:S(2)}) async-start(), calls=%async_computation.1 | async-start | bytes 1179648 | tf_op jit(solution)/shard_map/all_gather | solution.py:27
  105.8 26.8 %collective-permute-start.2 = (bf16[1024,512]{1,0:T(8,128)(2,1)}, bf16[1024,512]{1,0:T(8,128)(2,1)S(1)}, u32[]{:S(2)}, u32[]{:S(2)}) collective-permute-start(bf16[1024,512]{1,0:T(8,128)(2,1)} %all-gather.8.cloned.1.call-done), channel_id=1, source_target_pairs={{0,16},{8,24},{16,32},{24,40},{32,48},{40,56},{48,64},{56,72},{64,... | collective-permute-start | bytes 3145736 | tf_op jit(solution)/shard_map/ppermute | solution.py:10
  110.1 53.2 %collective-permute-start.3 = (bf16[1024,512]{1,0:T(8,128)(2,1)}, bf16[1024,512]{1,0:T(8,128)(2,1)S(1)}, u32[]{:S(2)}, u32[]{:S(2)}) collective-permute-start(bf16[1024,512]{1,0:T(8,128)(2,1)} %all-gather.8.cloned.1.call-done), channel_id=1, source_target_pairs={{16,0},{24,8},{32,16},{40,24},{48,32},{56,40},{64,48},{72,56},{80,... | collective-permute-start | bytes 3145736 | tf_op jit(solution)/shard_map/ppermute | solution.py:10
  165.3 158.3 %all-gather.12.cloned.1.call-start = ((), (), s32[]{:S(2)}) async-start(), calls=%async_computation.2 | async-start | bytes 1179648 | tf_op jit(solution)/shard_map/all_gather | solution.py:27
  190.7 76.3 %collective-permute-start.4 = (bf16[1024,512]{0,1:T(8,128)(2,1)}, bf16[1024,512]{0,1:T(8,128)(2,1)S(1)}, u32[]{:S(2)}, u32[]{:S(2)}) collective-permute-start(bf16[1024,512]{0,1:T(8,128)(2,1)} %all-gather.10.cloned.1.call-done), channel_id=1, source_target_pairs={{0,32},{8,40},{16,48},{24,56},{32,64},{40,72},{48,80},{56,88},{64,... | collective-permute-start | bytes 3145736 | tf_op jit(solution)/shard_map/ppermute | solution.py:10
  198.5 69.0 %collective-permute-start.5 = (bf16[1024,512]{0,1:T(8,128)(2,1)}, bf16[1024,512]{0,1:T(8,128)(2,1)S(1)}, u32[]{:S(2)}, u32[]{:S(2)}) collective-permute-start(bf16[1024,512]{0,1:T(8,128)(2,1)} %all-gather.10.cloned.1.call-done), channel_id=1, source_target_pairs={{32,0},{40,8},{48,16},{56,24},{64,32},{72,40},{80,48},{88,56},{96,... | collective-permute-start | bytes 3145736 | tf_op jit(solution)/shard_map/ppermute | solution.py:10
  269.5 116.9 %all-gather.14.cloned.1.call-start = ((), (), s32[]{:S(2)}) async-start(), calls=%async_computation.3 | async-start | bytes 1179648 | tf_op jit(solution)/shard_map/all_gather | solution.py:27
  323.7 25.7 %collective-permute-start.6 = (bf16[1024,512]{0,1:T(8,128)(2,1)}, bf16[1024,512]{0,1:T(8,128)(2,1)S(1)}, u32[]{:S(2)}, u32[]{:S(2)}) collective-permute-start(bf16[1024,512]{0,1:T(8,128)(2,1)} %all-gather.12.cloned.1.call-done), channel_id=1, source_target_pairs={{0,64},{8,72},{16,80},{24,88},{32,96},{40,104},{48,112},{56,120},{... | collective-permute-start | bytes 3145736 | tf_op jit(solution)/shard_map/ppermute | solution.py:10
  326.8 26.3 %collective-permute-start.7 = (bf16[1024,512]{0,1:T(8,128)(2,1)}, bf16[1024,512]{0,1:T(8,128)(2,1)S(1)}, u32[]{:S(2)}, u32[]{:S(2)}) collective-permute-start(bf16[1024,512]{0,1:T(8,128)(2,1)} %all-gather.12.cloned.1.call-done), channel_id=1, source_target_pairs={{64,0},{72,8},{80,16},{88,24},{96,32},{104,40},{112,48},{120,56},{... | collective-permute-start | bytes 3145736 | tf_op jit(solution)/shard_map/ppermute | solution.py:10
  355.2 117.4 %all-gather.16.cloned.1.call-start = ((), (), s32[]{:S(2)}) async-start(), calls=%async_computation.4 | async-start | bytes 1179648 | tf_op jit(solution)/shard_map/all_gather | solution.py:27
  386.4 26.6 %collective-permute-start.8 = (bf16[1024,512]{0,1:T(8,128)(2,1)}, bf16[1024,512]{0,1:T(8,128)(2,1)S(1)}, u32[]{:S(2)}, u32[]{:S(2)}) collective-permute-start(bf16[1024,512]{0,1:T(8,128)(2,1)} %all-gather.14.cloned.1.call-done), channel_id=1, source_target_pairs={{0,128},{8,136},{16,144},{24,152},{32,160},{40,168},{48,176},{56,1... | collective-permute-start | bytes 3145736 | tf_op jit(solution)/shard_map/ppermute | solution.py:10
  390.5 51.5 %collective-permute-start.9 = (bf16[1024,512]{0,1:T(8,128)(2,1)}, bf16[1024,512]{0,1:T(8,128)(2,1)S(1)}, u32[]{:S(2)}, u32[]{:S(2)}) collective-permute-start(bf16[1024,512]{0,1:T(8,128)(2,1)} %all-gather.14.cloned.1.call-done), channel_id=1, source_target_pairs={{128,0},{136,8},{144,16},{152,24},{160,32},{168,40},{176,48},{184,... | collective-permute-start | bytes 3145736 | tf_op jit(solution)/shard_map/ppermute | solution.py:10
  472.5 42.2 %collective-permute-start.10 = (bf16[1024,512]{0,1:T(8,128)(2,1)}, bf16[1024,512]{0,1:T(8,128)(2,1)S(1)}, u32[]{:S(2)}, u32[]{:S(2)}) collective-permute-start(bf16[1024,512]{0,1:T(8,128)(2,1)} %all-gather.16.cloned.1.call-done), channel_id=1, source_target_pairs={{0,256},{8,264},{16,272},{24,280},{32,288},{40,296},{48,304},{56,3... | collective-permute-start | bytes 3145736 | tf_op jit(solution)/shard_map/ppermute | solution.py:10
  479.7 51.0 %collective-permute-start.11 = (bf16[1024,512]{0,1:T(8,128)(2,1)}, bf16[1024,512]{0,1:T(8,128)(2,1)S(1)}, u32[]{:S(2)}, u32[]{:S(2)}) collective-permute-start(bf16[1024,512]{0,1:T(8,128)(2,1)} %all-gather.16.cloned.1.call-done), channel_id=1, source_target_pairs={{256,0},{264,8},{272,16},{280,24},{288,32},{296,40},{304,48},{312,... | collective-permute-start | bytes 3145736 | tf_op jit(solution)/shard_map/ppermute | solution.py:10
Sparse Core Ops, SparseCore 0:
  9.5 34.7 all-gather.17
  75.8 29.9 all-gather.7
  165.5 25.1 all-gather.9
  269.6 53.9 all-gather.11
  355.3 31.0 all-gather.13
  444.1 28.3 all-gather.15
where the time goes:
time: 540 us
  waiting for transfers between devices  464 us (86%)
  starting transfers between devices  37.5 us (7%)
  matrix products  24.1 us (4%)
  between operations  13.7 us (3%)
    ppermute x12, waiting for transfers between devices, shifted(): lax.ppermute(value, axis, [(source, source + steps) for source in range(i...  257 us
    all_gather x6, waiting for transfers between devices, body(): whole = lax.all_gather(current, 'cross', axis=0, tiled=True)  206 us
    ppermute x12, starting transfers between devices, shifted(): lax.ppermute(value, axis, [(source, source + steps) for source in range(i...  37.3 us
    dot_general x6, matrix products, body(): total = total - jnp.dot(up_mat, upper, preferred_element_type=jnp.float32)  11.5 us
  transfers between devices with their start and end apart: 18, of which 17 were waited for; matrix products, arithmetic and copies ran while one was open for 2% of the time, Pallas kernels for 0%

commit v1 on v0

--- a/solution.py
+++ b/solution.py
@@ -24,7 +24,8 @@
         own_mat = self_factor[level, 0]
         low_mat = lower_factor[level, 0]
         up_mat = upper_factor[level, 0]
-        whole = lax.all_gather(current, "cross", axis=0, tiled=True)
+        sent = jnp.stack([current] * lax.axis_size("cross"))
+        whole = jnp.concatenate(lax.all_to_all(sent, "cross", 0, 0), axis=0)
         lower, upper = reach_full(whole, dist)
         total = jnp.dot(own_mat, whole, preferred_element_type=jnp.float32)
         total = total - jnp.dot(low_mat, lower, preferred_element_type=jnp.float32)

time: 540 us -> 454 us (0.84)
  waiting for transfers between devices: 464 us -> 248 us
  blocking collectives: 0 us -> 124 us
  starting transfers between devices: 37.5 us -> 61.8 us
  between operations: 13.7 us -> 0.29 us
  matrix products: 24.1 us -> 13.8 us
    all_gather x6 -> x0, waiting for transfers between devices: 206 us -> none  [body(): whole = lax.all_gather(current, 'cross', axis=0, tiled=True)]
    all_to_all x0 -> x6, blocking collectives: none -> 124 us  [body(): whole = jnp.concatenate(lax.all_to_all(sent, 'cross', 0, 0), axis=0)]
    ppermute x12, starting transfers between devices: 37.3 us -> 61.8 us  [shifted(): lax.ppermute(value, axis, [(source, source + steps) for source in range(i...]
    ppermute x12, waiting for transfers between devices: 257 us -> 248 us  [shifted(): lax.ppermute(value, axis, [(source, source + steps) for source in range(i...]
    dot_general x6, matrix products: 9.96 us -> 2.69 us  [body(): total = jnp.dot(own_mat, whole, preferred_element_type=jnp.float32)]
  transfers between devices with their start and end apart: 18 -> 12, of which waited for: 17 -> 11; matrix products, arithmetic and copies ran while one was open for 2% -> 1% of each run, Pallas kernels for 0% -> 0%
where the time goes in v1:
time: 454 us; the launch traced here: 451 us
  waiting for transfers between devices  248 us (55%)
  blocking collectives  124 us (27%)
  starting transfers between devices  61.8 us (14%)
  matrix products  13.8 us (3%)
    ppermute x12, waiting for transfers between devices, shifted(): lax.ppermute(value, axis, [(source, source + steps) for source in range(i...  248 us
    all_to_all x6, blocking collectives, body(): whole = jnp.concatenate(lax.all_to_all(sent, 'cross', 0, 0), axis=0)  124 us
    ppermute x12, starting transfers between devices, shifted(): lax.ppermute(value, axis, [(source, source + steps) for source in range(i...  61.8 us
  transfers between devices with their start and end apart: 12, of which 11 were waited for; matrix products, arithmetic and copies ran while one was open for 1% of the time, Pallas kernels for 0%

profile of v1, /device:TPU:1, one launch (start us, length us, event | category | flops | bytes accessed | tf_op | source)
XLA Modules:
  0.0 450.7 jit_solution(2460205022453889421)
XLA Ops:
  0.0 1.1 stack.12
  1.1 24.5 %all_to_all.30 = bf16[8,128,512]{2,1,0:T(8,128)(2,1)S(1)} all-to-all(bf16[8,128,512]{2,1,0:T(8,128)(2,1)S(1)} %stack.12), channel_id=1, replica_groups=mesh['chain'=64,'cross'=8] {'cross'}, dimensions={0} | all-to-all | bytes 2097152 | tf_op jit(solution)/shard_map/all_to_all | solution.py:28
  25.6 1.3 collective-permute-start
  27.0 1.3 collective-permute-start.1
  28.6 20.0 %collective-permute-done = bf16[1024,512]{1,0:T(8,128)(2,1)S(1)} collective-permute-done((bf16[1024,512]{1,0:T(8,128)(2,1)S(1)}, bf16[1024,512]{1,0:T(8,128)(2,1)S(1)}, u32[]{:S(2)}, u32[]{:S(2)}) %collective-permute-start) | collective-permute-done | bytes 1048608 | tf_op jit(solution)/shard_map/ppermute | solution.py:10
  48.6 0.3 convolution_subtract_fusion.11
  48.9 3.5 collective-permute-done.1
  52.5 1.3 fusion
  53.8 19.4 %all_to_all.31 = bf16[8,128,512]{2,1,0:T(8,128)(2,1)S(1)} all-to-all(bf16[8,128,512]{2,1,0:T(8,128)(2,1)S(1)} %stack.13), channel_id=1, replica_groups=mesh['chain'=64,'cross'=8] {'cross'}, dimensions={0} | all-to-all | bytes 2097152 | tf_op jit(solution)/shard_map/all_to_all | solution.py:28
  73.3 6.7 %collective-permute-start.2 = (bf16[1024,512]{1,0:T(8,128)(2,1)S(1)}, bf16[1024,512]{1,0:T(8,128)(2,1)S(1)}, u32[]{:S(2)}, u32[]{:S(2)}) collective-permute-start(bf16[1024,512]{1,0:T(8,128)(2,1)S(1)} %bitcast.94), channel_id=1, source_target_pairs={{0,16},{8,24},{16,32},{24,40},{32,48},{40,56},{48,64},{56,72},{64,... | collective-permute-start | bytes 3145736 | tf_op jit(solution)/shard_map/ppermute | solution.py:10
  79.9 1.3 collective-permute-start.3
  81.2 0.5 fusion.29
  81.7 19.6 %collective-permute-done.2 = bf16[1024,512]{1,0:T(8,128)(2,1)S(1)} collective-permute-done((bf16[1024,512]{1,0:T(8,128)(2,1)S(1)}, bf16[1024,512]{1,0:T(8,128)(2,1)S(1)}, u32[]{:S(2)}, u32[]{:S(2)}) %collective-permute-start.2) | collective-permute-done | bytes 1048608 | tf_op jit(solution)/shard_map/ppermute | solution.py:10
  101.3 0.5 convolution_subtract_fusion.9
  101.8 25.2 %collective-permute-done.3 = bf16[1024,512]{1,0:T(8,128)(2,1)S(1)} collective-permute-done((bf16[1024,512]{1,0:T(8,128)(2,1)S(1)}, bf16[1024,512]{1,0:T(8,128)(2,1)S(1)}, u32[]{:S(2)}, u32[]{:S(2)}) %collective-permute-start.3) | collective-permute-done | bytes 1048608 | tf_op jit(solution)/shard_map/ppermute | solution.py:10
  127.0 1.4 fusion.10
  128.6 21.5 %all_to_all.32 = bf16[8,128,512]{2,1,0:T(8,128)(2,1)S(1)} all-to-all(bf16[8,128,512]{2,1,0:T(8,128)(2,1)S(1)} %stack.14), channel_id=1, replica_groups=mesh['chain'=64,'cross'=8] {'cross'}, dimensions={0} | all-to-all | bytes 2097152 | tf_op jit(solution)/shard_map/all_to_all | solution.py:28
  150.1 5.9 %collective-permute-start.4 = (bf16[1024,512]{1,0:T(8,128)(2,1)S(1)}, bf16[1024,512]{1,0:T(8,128)(2,1)S(1)}, u32[]{:S(2)}, u32[]{:S(2)}) collective-permute-start(bf16[1024,512]{1,0:T(8,128)(2,1)S(1)} %bitcast.97), channel_id=1, source_target_pairs={{0,32},{8,40},{16,48},{24,56},{32,64},{40,72},{48,80},{56,88},{64,... | collective-permute-start | bytes 3145736 | tf_op jit(solution)/shard_map/ppermute | solution.py:10
  156.0 1.3 collective-permute-start.5
  157.3 0.5 fusion.25
  157.8 66.8 %collective-permute-done.4 = bf16[1024,512]{1,0:T(8,128)(2,1)S(1)} collective-permute-done((bf16[1024,512]{1,0:T(8,128)(2,1)S(1)}, bf16[1024,512]{1,0:T(8,128)(2,1)S(1)}, u32[]{:S(2)}, u32[]{:S(2)}) %collective-permute-start.4) | collective-permute-done | bytes 1048608 | tf_op jit(solution)/shard_map/ppermute | solution.py:10
  224.6 0.5 convolution_subtract_fusion.7
  225.0 1.4 fusion.9
  226.7 19.4 %all_to_all.33 = bf16[8,128,512]{2,1,0:T(8,128)(2,1)S(1)} all-to-all(bf16[8,128,512]{2,1,0:T(8,128)(2,1)S(1)} %stack.15), channel_id=1, replica_groups=mesh['chain'=64,'cross'=8] {'cross'}, dimensions={0} | all-to-all | bytes 2097152 | tf_op jit(solution)/shard_map/all_to_all | solution.py:28
  246.1 24.4 %collective-permute-start.6 = (bf16[1024,512]{1,0:T(8,128)(2,1)S(1)}, bf16[1024,512]{1,0:T(8,128)(2,1)S(1)}, u32[]{:S(2)}, u32[]{:S(2)}) collective-permute-start(bf16[1024,512]{1,0:T(8,128)(2,1)S(1)} %bitcast.100), channel_id=1, source_target_pairs={{0,64},{8,72},{16,80},{24,88},{32,96},{40,104},{48,112},{56,120},{... | collective-permute-start | bytes 3145736 | tf_op jit(solution)/shard_map/ppermute | solution.py:10
  270.5 1.3 collective-permute-start.7
  271.8 0.5 fusion.21
  272.3 19.5 %collective-permute-done.6 = bf16[1024,512]{1,0:T(8,128)(2,1)S(1)} collective-permute-done((bf16[1024,512]{1,0:T(8,128)(2,1)S(1)}, bf16[1024,512]{1,0:T(8,128)(2,1)S(1)}, u32[]{:S(2)}, u32[]{:S(2)}) %collective-permute-start.6) | collective-permute-done | bytes 1048608 | tf_op jit(solution)/shard_map/ppermute | solution.py:10
  291.9 0.5 convolution_subtract_fusion.5
  292.3 3.4 collective-permute-done.7
  295.8 1.4 fusion.8
  297.4 19.7 %all_to_all.34 = bf16[8,128,512]{2,1,0:T(8,128)(2,1)S(1)} all-to-all(bf16[8,128,512]{2,1,0:T(8,128)(2,1)S(1)} %stack.16), channel_id=1, replica_groups=mesh['chain'=64,'cross'=8] {'cross'}, dimensions={0} | all-to-all | bytes 2097152 | tf_op jit(solution)/shard_map/all_to_all | solution.py:28
  317.1 10.5 %collective-permute-start.8 = (bf16[1024,512]{1,0:T(8,128)(2,1)S(1)}, bf16[1024,512]{1,0:T(8,128)(2,1)S(1)}, u32[]{:S(2)}, u32[]{:S(2)}) collective-permute-start(bf16[1024,512]{1,0:T(8,128)(2,1)S(1)} %bitcast.103), channel_id=1, source_target_pairs={{0,128},{8,136},{16,144},{24,152},{32,160},{40,168},{48,176},{56,1... | collective-permute-start | bytes 3145736 | tf_op jit(solution)/shard_map/ppermute | solution.py:10
  327.6 1.3 collective-permute-start.9
  328.9 0.5 fusion.17
  329.4 19.6 %collective-permute-done.8 = bf16[1024,512]{1,0:T(8,128)(2,1)S(1)} collective-permute-done((bf16[1024,512]{1,0:T(8,128)(2,1)S(1)}, bf16[1024,512]{1,0:T(8,128)(2,1)S(1)}, u32[]{:S(2)}, u32[]{:S(2)}) %collective-permute-start.8) | collective-permute-done | bytes 1048608 | tf_op jit(solution)/shard_map/ppermute | solution.py:10
  349.0 0.5 convolution_subtract_fusion.3
  349.5 23.4 %collective-permute-done.9 = bf16[1024,512]{1,0:T(8,128)(2,1)S(1)} collective-permute-done((bf16[1024,512]{1,0:T(8,128)(2,1)S(1)}, bf16[1024,512]{1,0:T(8,128)(2,1)S(1)}, u32[]{:S(2)}, u32[]{:S(2)}) %collective-permute-start.9) | collective-permute-done | bytes 1048608 | tf_op jit(solution)/shard_map/ppermute | solution.py:10
  372.8 1.4 fusion.7
  374.5 19.7 %all_to_all.35 = bf16[8,128,512]{2,1,0:T(8,128)(2,1)S(1)} all-to-all(bf16[8,128,512]{2,1,0:T(8,128)(2,1)S(1)} %stack.17), channel_id=1, replica_groups=mesh['chain'=64,'cross'=8] {'cross'}, dimensions={0} | all-to-all | bytes 2097152 | tf_op jit(solution)/shard_map/all_to_all | solution.py:28
  394.2 5.3 %collective-permute-start.10 = (bf16[1024,512]{1,0:T(8,128)(2,1)S(1)}, bf16[1024,512]{1,0:T(8,128)(2,1)S(1)}, u32[]{:S(2)}, u32[]{:S(2)}) collective-permute-start(bf16[1024,512]{1,0:T(8,128)(2,1)S(1)} %bitcast.106), channel_id=1, source_target_pairs={{0,256},{8,264},{16,272},{24,280},{32,288},{40,296},{48,304},{56,3... | collective-permute-start | bytes 3145736 | tf_op jit(solution)/shard_map/ppermute | solution.py:10
  399.5 1.3 collective-permute-start.11
  400.8 0.5 fusion.13
  401.3 42.4 %collective-permute-done.10 = bf16[1024,512]{1,0:T(8,128)(2,1)S(1)} collective-permute-done((bf16[1024,512]{1,0:T(8,128)(2,1)S(1)}, bf16[1024,512]{1,0:T(8,128)(2,1)S(1)}, u32[]{:S(2)}, u32[]{:S(2)}) %collective-permute-start.10) | collective-permute-done | bytes 1048608 | tf_op jit(solution)/shard_map/ppermute | solution.py:10
  443.6 0.5 convolution_subtract_fusion.1
  444.1 4.4 collective-permute-done.11
  448.5 1.4 fusion.6
  449.9 0.8 copy.9
  (15 shorter events, 1.2 us)
Async XLA Ops:
  0.0 28.3 %copy-start.1 = (bf16[6,1,128,1024]{3,2,1,0:T(8,128)(2,1)S(1)}, bf16[6,1,128,1024]{3,2,1,0:T(8,128)(2,1)}, u32[]{:S(2)}) copy-start(bf16[6,1,128,1024]{3,2,1,0:T(8,128)(2,1)} %param.5) | copy-start | bytes 4718596
  1.1 47.5 %copy-start = (bf16[6,1,128,1024]{3,2,1,0:T(8,128)(2,1)S(1)}, bf16[6,1,128,1024]{3,2,1,0:T(8,128)(2,1)}, u32[]{:S(2)}) copy-start(bf16[6,1,128,1024]{3,2,1,0:T(8,128)(2,1)} %param.6) | copy-start | bytes 4718596
  25.6 23.0 %collective-permute-start = (bf16[1024,512]{1,0:T(8,128)(2,1)S(1)}, bf16[1024,512]{1,0:T(8,128)(2,1)S(1)}, u32[]{:S(2)}, u32[]{:S(2)}) collective-permute-start(bf16[1024,512]{1,0:T(8,128)(2,1)S(1)} %bitcast.91), channel_id=1, source_target_pairs={{0,8},{8,16},{16,24},{24,32},{32,40},{40,48},{48,56},{56,64},{64,7... | collective-permute-start | bytes 3145736 | tf_op jit(solution)/shard_map/ppermute | solution.py:10
  27.0 25.5 %collective-permute-start.1 = (bf16[1024,512]{1,0:T(8,128)(2,1)S(1)}, bf16[1024,512]{1,0:T(8,128)(2,1)S(1)}, u32[]{:S(2)}, u32[]{:S(2)}) collective-permute-start(bf16[1024,512]{1,0:T(8,128)(2,1)S(1)} %bitcast.92), channel_id=1, source_target_pairs={{8,0},{16,8},{24,16},{32,24},{40,32},{48,40},{56,48},{64,56},{72,6... | collective-permute-start | bytes 3145736 | tf_op jit(solution)/shard_map/ppermute | solution.py:10
  73.3 28.0 %collective-permute-start.2 = (bf16[1024,512]{1,0:T(8,128)(2,1)S(1)}, bf16[1024,512]{1,0:T(8,128)(2,1)S(1)}, u32[]{:S(2)}, u32[]{:S(2)}) collective-permute-start(bf16[1024,512]{1,0:T(8,128)(2,1)S(1)} %bitcast.94), channel_id=1, source_target_pairs={{0,16},{8,24},{16,32},{24,40},{32,48},{40,56},{48,64},{56,72},{64,... | collective-permute-start | bytes 3145736 | tf_op jit(solution)/shard_map/ppermute | solution.py:10
  79.9 47.0 %collective-permute-start.3 = (bf16[1024,512]{1,0:T(8,128)(2,1)S(1)}, bf16[1024,512]{1,0:T(8,128)(2,1)S(1)}, u32[]{:S(2)}, u32[]{:S(2)}) collective-permute-start(bf16[1024,512]{1,0:T(8,128)(2,1)S(1)} %bitcast.95), channel_id=1, source_target_pairs={{16,0},{24,8},{32,16},{40,24},{48,32},{56,40},{64,48},{72,56},{80,... | collective-permute-start | bytes 3145736 | tf_op jit(solution)/shard_map/ppermute | solution.py:10
  150.1 74.4 %collective-permute-start.4 = (bf16[1024,512]{1,0:T(8,128)(2,1)S(1)}, bf16[1024,512]{1,0:T(8,128)(2,1)S(1)}, u32[]{:S(2)}, u32[]{:S(2)}) collective-permute-start(bf16[1024,512]{1,0:T(8,128)(2,1)S(1)} %bitcast.97), channel_id=1, source_target_pairs={{0,32},{8,40},{16,48},{24,56},{32,64},{40,72},{48,80},{56,88},{64,... | collective-permute-start | bytes 3145736 | tf_op jit(solution)/shard_map/ppermute | solution.py:10
  156.0 69.0 %collective-permute-start.5 = (bf16[1024,512]{1,0:T(8,128)(2,1)S(1)}, bf16[1024,512]{1,0:T(8,128)(2,1)S(1)}, u32[]{:S(2)}, u32[]{:S(2)}) collective-permute-start(bf16[1024,512]{1,0:T(8,128)(2,1)S(1)} %bitcast.98), channel_id=1, source_target_pairs={{32,0},{40,8},{48,16},{56,24},{64,32},{72,40},{80,48},{88,56},{96,... | collective-permute-start | bytes 3145736 | tf_op jit(solution)/shard_map/ppermute | solution.py:10
  246.1 45.7 %collective-permute-start.6 = (bf16[1024,512]{1,0:T(8,128)(2,1)S(1)}, bf16[1024,512]{1,0:T(8,128)(2,1)S(1)}, u32[]{:S(2)}, u32[]{:S(2)}) collective-permute-start(bf16[1024,512]{1,0:T(8,128)(2,1)S(1)} %bitcast.100), channel_id=1, source_target_pairs={{0,64},{8,72},{16,80},{24,88},{32,96},{40,104},{48,112},{56,120},{... | collective-permute-start | bytes 3145736 | tf_op jit(solution)/shard_map/ppermute | solution.py:10
  270.5 25.2 %collective-permute-start.7 = (bf16[1024,512]{1,0:T(8,128)(2,1)S(1)}, bf16[1024,512]{1,0:T(8,128)(2,1)S(1)}, u32[]{:S(2)}, u32[]{:S(2)}) collective-permute-start(bf16[1024,512]{1,0:T(8,128)(2,1)S(1)} %bitcast.101), channel_id=1, source_target_pairs={{64,0},{72,8},{80,16},{88,24},{96,32},{104,40},{112,48},{120,56},{... | collective-permute-start | bytes 3145736 | tf_op jit(solution)/shard_map/ppermute | solution.py:10
  317.1 31.9 %collective-permute-start.8 = (bf16[1024,512]{1,0:T(8,128)(2,1)S(1)}, bf16[1024,512]{1,0:T(8,128)(2,1)S(1)}, u32[]{:S(2)}, u32[]{:S(2)}) collective-permute-start(bf16[1024,512]{1,0:T(8,128)(2,1)S(1)} %bitcast.103), channel_id=1, source_target_pairs={{0,128},{8,136},{16,144},{24,152},{32,160},{40,168},{48,176},{56,1... | collective-permute-start | bytes 3145736 | tf_op jit(solution)/shard_map/ppermute | solution.py:10
  327.6 45.2 %collective-permute-start.9 = (bf16[1024,512]{1,0:T(8,128)(2,1)S(1)}, bf16[1024,512]{1,0:T(8,128)(2,1)S(1)}, u32[]{:S(2)}, u32[]{:S(2)}) collective-permute-start(bf16[1024,512]{1,0:T(8,128)(2,1)S(1)} %bitcast.104), channel_id=1, source_target_pairs={{128,0},{136,8},{144,16},{152,24},{160,32},{168,40},{176,48},{184,... | collective-permute-start | bytes 3145736 | tf_op jit(solution)/shard_map/ppermute | solution.py:10
  394.2 49.4 %collective-permute-start.10 = (bf16[1024,512]{1,0:T(8,128)(2,1)S(1)}, bf16[1024,512]{1,0:T(8,128)(2,1)S(1)}, u32[]{:S(2)}, u32[]{:S(2)}) collective-permute-start(bf16[1024,512]{1,0:T(8,128)(2,1)S(1)} %bitcast.106), channel_id=1, source_target_pairs={{0,256},{8,264},{16,272},{24,280},{32,288},{40,296},{48,304},{56,3... | collective-permute-start | bytes 3145736 | tf_op jit(solution)/shard_map/ppermute | solution.py:10
  399.5 49.0 %collective-permute-start.11 = (bf16[1024,512]{1,0:T(8,128)(2,1)S(1)}, bf16[1024,512]{1,0:T(8,128)(2,1)S(1)}, u32[]{:S(2)}, u32[]{:S(2)}) collective-permute-start(bf16[1024,512]{1,0:T(8,128)(2,1)S(1)} %bitcast.107), channel_id=1, source_target_pairs={{256,0},{264,8},{272,16},{280,24},{288,32},{296,40},{304,48},{312,... | collective-permute-start | bytes 3145736 | tf_op jit(solution)/shard_map/ppermute | solution.py:10
